TPU v7x, 32 devices: a whole 2x2x4 slice. The times are simulated.
32 devices in a mesh: stream: 4 (over y, core), cross: 2 (over x), gore: 4 (over z).
Axes of the slice: x: 2, y: 2, z: 4, core: 2. Of those that a mesh axis runs over, the one named last changes fastest.
Arguments:
- density: float32 [16, 8, 512], P('stream', 'cross', 'gore'), may hold values from 1 to 2
- momentum_energy: float32 [4, 16, 8, 512], P(None, 'stream', 'cross', 'gore'), may hold values from -6 to 6
- viscosity: float32 [16, 8, 512], P('stream', 'cross', 'gore'), may hold values from 0.02 to 0.15
- records: float32 [8, 2048, 128], P(None, ('stream', 'cross', 'gore')), may hold values from -6 to 6
- cell_ids: int32 [2048, 128], P(('stream', 'cross', 'gore')), may hold values from 0 to 2047
- routes: int32 [2048, 1], P(('stream', 'cross', 'gore')), may hold values from 0 to 7; in each aligned block of 64 rows (0 to 63, 64 to 127, ...) at most 16 rows name the same one
- lengths: int32 [2048], P(('stream', 'cross', 'gore')), may hold values from 1 to 128, 163840 in all
Outputs:
- new_state: float32 [5, 16, 8, 512], P(None, 'stream', 'cross', 'gore')
- face_loads: float32 [3, 2048, 128], P(None, ('stream', 'cross', 'gore'))
Inputs may be any that keep to these rules, and one draw needn't show every extreme that they name: `routes`: among the 64 tiles of one device no fluid block is named more than 16 times, and some block exactly 16 times. `lengths`: some tile is full.
All inputs are finite; a program needn't handle non-finite values. No bound on the sum of `lengths` on one device may be relied on, other than what follows from the above.
Results may differ from a plain program's by a relative error of at most 0.0003.
Values sent between devices are 32-bit elements; how exact they have to be, the bound alone decides.
No kernel may reach another device: no remote copies, remote signals or barrier semaphores. Data moves between devices by JAX's collectives and lax.ppermute only.
A program may use at most 64 MiB of HBM per device.

v0:
```python
import jax
import jax.numpy as jnp
from jax import lax
from jax.sharding import PartitionSpec as P

SIDES = (("stream", 1), ("cross", 2), ("gore", 3))


def face_halo(block):
    wide = block
    for axis, dim in SIDES:
        count = lax.axis_size(axis)
        index = lax.axis_index(axis)
        odd = index % 2 == 1
        extent = block.shape[dim]
        last = lax.slice_in_dim(block, extent - 1, None, axis=dim)
        first = lax.slice_in_dim(block, 0, 1, axis=dim)
        pairs_a = [(i, i ^ 1) for i in range(count) if i ^ 1 < count]
        pairs_b = [
            (i, j)
            for i in range(1, count)
            for j in (i - 1, i + 1)
            if j >= 1 and j < count and (min(i, j) % 2 == 1)
        ]
        from_a = lax.ppermute(jnp.where(odd, first, last), axis, pairs_a)
        if pairs_b:
            from_b = lax.ppermute(jnp.where(odd, last, first), axis, pairs_b)
        else:
            from_b = jnp.zeros_like(from_a)
        low = jnp.where(odd, from_a, from_b)
        high = jnp.where(odd, from_b, from_a)
        widths = [(0, 0)] + [(1, 1) if d < dim else (0, 0) for d in range(1, 4)]
        wide = jnp.concatenate([jnp.pad(low, widths), wide, jnp.pad(high, widths)], axis=dim)
    return wide


def harmonic(first_visc, second_visc):
    summed = first_visc + second_visc
    denominator = jnp.where(summed > 0, summed, 1.0)
    return 2.0 * first_visc * second_visc / denominator


def shifted(values, leading, spatial, offset):
    value_portions = [slice(None)] * leading
    for position in range(3):
        extent = values.shape[leading + position]
        if position == spatial:
            value_portions.append(slice(1 + offset, extent - 1 + offset))
        else:
            value_portions.append(slice(1, extent - 1))
    return values[tuple(value_portions)]


def viscous(field, visc):
    centre = shifted(field, 1, 0, 0)
    centre_visc = shifted(visc, 0, 0, 0)
    change = jnp.zeros_like(centre)
    for spatial in range(3):
        for offset in (1, -1):
            face_visc = harmonic(centre_visc, shifted(visc, 0, spatial, offset))
            change = change + face_visc[None] * (shifted(field, 1, spatial, offset) - centre)
    return change


def split_high(values):
    scaled = values * jnp.float32(65537.0)
    high = scaled - (scaled - values)
    return (high, values - high)


def three_bf16(values):
    first, rest = split_high(values)
    second, third = split_high(rest)
    return tuple((part.astype(jnp.bfloat16) for part in (first, second, third)))


def exact_dot(spec, values, onehot, values_first):
    stacked = jnp.stack(three_bf16(values), 0)
    left, right = spec.split("->")[0].split(",")
    output = spec.split("->")[1]
    if values_first:
        terms = jnp.einsum(
            "k" + left + "," + right + "->k" + output,
            stacked,
            onehot,
            preferred_element_type=jnp.float32,
        )
    else:
        terms = jnp.einsum(
            left + ",k" + right + "->k" + output,
            onehot,
            stacked,
            preferred_element_type=jnp.float32,
        )
    return terms[0] + terms[1] + terms[2]


def shards(density, momentum_energy, viscosity, records, cell_ids, routes, lengths):
    fluid_state = jnp.concatenate([density[None], momentum_energy], 0)
    cells_x, cells_y, vertical_cells = density.shape
    plane_count = cells_x * cells_y
    tile_count = records.shape[1]
    row_count = records.shape[2]
    blocks = lax.axis_size("stream") * lax.axis_size("cross")
    capacity = max(2, 2 * tile_count // blocks)
    slot_total = blocks * capacity
    faces = slot_total * row_count
    live_rows = lax.broadcasted_iota(jnp.int32, (tile_count, row_count), 1) < lengths[:, None]
    masked_values = jnp.where(live_rows[None], records, 0.0)
    target = routes[:, 0]
    onehot = (target[:, None] == lax.broadcasted_iota(jnp.int32, (tile_count, blocks), 1)).astype(
        jnp.float32
    )
    lower = (
        lax.broadcasted_iota(jnp.int32, (tile_count, tile_count), 1)
        < lax.broadcasted_iota(jnp.int32, (tile_count, tile_count), 0)
    ).astype(jnp.float32)
    before = jnp.dot(
        lower, onehot, precision=lax.Precision.HIGHEST, preferred_element_type=jnp.float32
    )
    slot_rank = jnp.sum(before * onehot, axis=1).astype(jnp.int32)
    slot_index = target * capacity + slot_rank
    placement_plan = (
        slot_index[:, None] == lax.broadcasted_iota(jnp.int32, (tile_count, slot_total), 1)
    ).astype(jnp.float32)
    payload = jnp.concatenate(
        [jnp.abs(masked_values[0:1]), masked_values[1:5], cell_ids.astype(jnp.float32)[None]], 0
    )
    outbound = jnp.einsum("ts,ctr->csr", placement_plan, payload, precision=lax.Precision.HIGHEST)
    arrived = lax.all_to_all(outbound, ("stream", "cross"), split_axis=1, concat_axis=1, tiled=True)
    outbound, state_and_visc = lax.optimization_barrier(
        (outbound, jnp.concatenate([fluid_state, viscosity[None]], 0))
    )
    state_visc = face_halo(state_and_visc)
    state_pad = state_visc[0:5]
    visc_pad = state_visc[5]
    cells = jnp.round(arrived[5]).astype(jnp.int32).reshape(faces)
    plane = cells // vertical_cells
    depth = cells % vertical_cells
    depth_hot = depth[:, None] == lax.broadcasted_iota(jnp.int32, (faces, vertical_cells), 1)
    plane_rows = plane[None, :] == lax.broadcasted_iota(jnp.int32, (plane_count, faces), 0)
    spread = jnp.where(plane_rows[None], arrived[0:5].reshape(5, 1, faces), 0.0)
    source = jnp.einsum(
        "cpf,fd->cpd", spread, depth_hot.astype(jnp.float32), precision=lax.Precision.HIGHEST
    )
    source = source.reshape(5, cells_x, cells_y, vertical_cells)
    middle = shifted(state_pad, 1, 0, 0) + viscous(state_pad, visc_pad) + source
    middle_pad = face_halo(middle)
    new_state = middle + viscous(middle_pad, visc_pad)
    flat_state = new_state.reshape(5, plane_count, vertical_cells)
    kinetic = (
        flat_state[1] * flat_state[1]
        + flat_state[2] * flat_state[2]
        + flat_state[3] * flat_state[3]
    )
    pressure = 0.4 * (flat_state[4] - 0.5 * kinetic / flat_state[0])
    picked = exact_dot("fd,dp->fp", pressure.T, depth_hot.astype(jnp.bfloat16), False)
    plane_cols = plane[:, None] == lax.broadcasted_iota(jnp.int32, (faces, plane_count), 1)
    face_pressure = jnp.sum(jnp.where(plane_cols, picked, 0.0), axis=1)
    returned = lax.all_to_all(
        face_pressure.reshape(1, slot_total, row_count),
        ("stream", "cross"),
        split_axis=1,
        concat_axis=1,
        tiled=True,
    )
    home_pressure = jnp.einsum(
        "ts,sr->tr", placement_plan, returned[0], precision=lax.Precision.HIGHEST
    )
    face_loads = masked_values[5:8] * home_pressure[None]
    return (new_state, face_loads)


def solution(mesh):
    placed = (
        P("stream", "cross", "gore"),
        P(None, "stream", "cross", "gore"),
        P("stream", "cross", "gore"),
        P(None, ("stream", "cross", "gore"), None),
        P(("stream", "cross", "gore"), None),
        P(("stream", "cross", "gore"), None),
        P(("stream", "cross", "gore")),
    )
    return jax.shard_map(
        shards,
        mesh=mesh,
        in_specs=placed,
        out_specs=(P(None, "stream", "cross", "gore"), P(None, ("stream", "cross", "gore"), None)),
        check_vma=False,
    )
```

profile of v0, /device:TPU:0, one launch (start us, length us, event | category | flops | bytes accessed | tf_op | source)
XLA Modules:
  0.0 50.3 jit_solution(16968767982298639690)
XLA Ops:
  0.6 0.7 %iota_compare_fusion.6 = pred[64,128]{1,0:T(8,128)(4,1)S(1)} fusion(s32[64]{0:T(128)} %param.13), kind=kLoop, calls=%fused_computation.133 | loop fusion | flops 8192 | bytes 8448 | tf_op jit(solution)/shard_map/lt | solution.py:108
  1.4 1.0 %broadcast_select_fusion = f32[8,64,128]{2,1,0:T(8,128)S(1)} fusion(f32[8,64,128]{2,1,0:T(8,128)} %param.10, pred[64,128]{1,0:T(8,128)(4,1)S(1)} %iota_compare_fusion.6), kind=kLoop, calls=%fused_computation.26 | loop fusion | flops 65536 | bytes 532480 | tf_op jit(solution)/shard_map/jit(_where)/select_n | solution.py:109
  2.4 0.8 %convert_bitcast_fusion = f32[1,64,128]{2,1,0:T(8,128)S(1)} fusion(s32[64,128]{1,0:T(8,128)} %param.11), kind=kLoop, calls=%fused_computation.132 | loop fusion | flops 8192 | bytes 65536 | tf_op jit(solution)/shard_map/broadcast_in_dim | solution.py:127
  3.1 0.9 %fusion.10 = f32[64]{0:T(128)S(1)} fusion(s32[64]{0:T(128)} %bitcast.99), kind=kOutput, calls=%fused_computation.12 | convolution fusion | flops 71616 | bytes 512 | tf_op jit(solution)/shard_map/dot_general | solution.py:118
  4.0 0.7 %fusion.92 = s32[64]{0:T(128)S(1)} fusion(f32[64]{0:T(128)S(1)} %fusion.10, s32[64,1]{0,1:T(1,128)} %param.12), kind=kLoop, calls=%fused_computation.194 | loop fusion | flops 192 | bytes 768 | tf_op jit(solution)/shard_map/eq | solution.py:124
  4.7 0.5 %convolution_bitcast_fusion.1 = f32[6,128,128]{1,2,0:T(8,128)S(1)} fusion(f32[1,64,128]{2,1,0:T(8,128)S(1)} %convert_bitcast_fusion, f32[4,64,128]{2,1,0:T(8,128)S(1)} %slice.230, f32[1,64,128]{2,1,0:T(8,128)S(1)} %slice_abs_fusion, s32[64]{0:T(128)S(1)} %fusion.92), kind=kOutput, calls=%fused_computation.10 | convolution fusion | flops 75603968 | bytes 590080 | tf_op jit(solution)/shard_map/ts,ctr->csr/dot_general | solution.py:129
  5.2 1.0 %copy.11 = f32[6,128,128]{2,0,1:T(8,128)} copy(f32[6,128,128]{1,2,0:T(8,128)S(1)} %convolution_bitcast_fusion.1) | data formatting | bytes 786432 | tf_op jit(solution)/shard_map/ts,ctr->csr/transpose | solution.py:129
  6.2 5.2 %all-to-all-start = ((f32[6,128,128]{2,0,1:T(8,128)}), f32[6,128,128]{2,0,1:T(8,128)S(1)}, u32[]{:S(2)}, u32[]{:S(2)}) async-start(f32[6,128,128]{2,0,1:T(8,128)} %copy.11), calls=%async_computation | async-start | bytes 1048576 | tf_op jit(solution)/shard_map/all_to_all | solution.py:130
  11.4 0.8 %pad_maximum_fusion.6 = f32[6,4,4,128]{3,2,1,0:T(4,128)S(1)} fusion(f32[1,4,4,128]{3,2,1,0:T(4,128)} %bitcast.97, f32[4,4,4,128]{3,2,1,0:T(4,128)} %param.8, f32[1,4,4,128]{3,2,1,0:T(4,128)} %bitcast.98), kind=kLoop, calls=%fused_computation.44 | loop fusion | flops 24576 | bytes 98304 | tf_op jit(solution)/shard_map/concatenate | solution.py:132
  12.3 0.7 %collective-permute-start.1 = (f32[6,4,4,1]{3,2,1,0:T(4,128)S(1)}, f32[6,4,4,1]{3,2,1,0:T(4,128)S(1)}, u32[]{:S(2)}, u32[]{:S(2)}) collective-permute-start(f32[6,4,4,1]{3,2,1,0:T(4,128)S(1)} %get-tuple-element.18), channel_id=1, source_target_pairs={{1,2},{2,1},{5,6},{6,5},{9,10},{10,9},{13,14},{14,13},{17,18},{18,... | collective-permute-start | bytes 1160 | tf_op jit(solution)/shard_map/ppermute | solution.py:27
  12.9 4.5 %collective-permute-start = (f32[6,4,4,1]{3,2,1,0:T(4,128)S(1)}, f32[6,4,4,1]{3,2,1,0:T(4,128)S(1)}, u32[]{:S(2)}, u32[]{:S(2)}) collective-permute-start(f32[6,4,4,1]{3,2,1,0:T(4,128)S(1)} %get-tuple-element.19), channel_id=1, source_target_pairs={{0,1},{1,0},{2,3},{3,2},{4,5},{5,4},{6,7},{7,6},{8,9},{9,8},{10,11... | collective-permute-start | bytes 1160 | tf_op jit(solution)/shard_map/ppermute | solution.py:25
  17.4 2.1 %collective-permute-start.2 = (f32[6,4,1,128]{3,2,1,0:T(1,128)S(1)}, f32[6,4,1,128]{3,2,1,0:T(1,128)S(1)}, u32[]{:S(2)}, u32[]{:S(2)}) collective-permute-start(f32[6,4,1,128]{3,2,1,0:T(1,128)S(1)} %broadcast_select_fusion.3), channel_id=1, source_target_pairs={{0,4},{4,0},{1,5},{5,1},{2,6},{6,2},{3,7},{7,3},{8,12},{12,8},{9,1... | collective-permute-start | bytes 36872 | tf_op jit(solution)/shard_map/ppermute | solution.py:25
  19.5 0.7 %collective-permute-start.4 = (f32[6,1,4,128]{3,2,1,0:T(4,128)S(1)}, f32[6,1,4,128]{3,2,1,0:T(4,128)S(1)}, u32[]{:S(2)}, u32[]{:S(2)}) collective-permute-start(f32[6,1,4,128]{3,2,1,0:T(4,128)S(1)} %get-tuple-element.17), channel_id=1, source_target_pairs={{8,16},{16,8},{9,17},{17,9},{10,18},{18,10},{11,19},{19,11},{12,20... | collective-permute-start | bytes 36872 | tf_op jit(solution)/shard_map/ppermute | solution.py:27
  20.3 0.4 collective-permute-done.3
  20.7 0.5 collective-permute-done.2
  21.3 0.1 fusion.21
  21.6 0.1 iota_compare_fusion.2
  21.8 0.5 fusion.103
  22.3 4.0 %fusion.2 = f32[5,16,128]{2,1,0:T(8,128)S(1)} fusion(s32[16384]{0:T(1024)S(1)} %get-tuple-element.9, f32[5,16,16384]{2,1,0:T(8,128)S(1)} %fusion.103), kind=kOutput, calls=%fused_computation.3 | convolution fusion | flops 2015363072 | bytes 5349376 | tf_op jit(solution)/shard_map/cpf,fd->cpd/dot_general | solution.py:143
  26.3 0.2 fusion.46
  26.6 0.7 %collective-permute-start.8 = (f32[5,4,4,1]{3,2,1,0:T(4,128)S(1)}, f32[5,4,4,1]{3,2,1,0:T(4,128)S(1)}, u32[]{:S(2)}, u32[]{:S(2)}) collective-permute-start(f32[5,4,4,1]{3,2,1,0:T(4,128)S(1)} %get-tuple-element.22), channel_id=1, source_target_pairs={{1,2},{2,1},{5,6},{6,5},{9,10},{10,9},{13,14},{14,13},{17,18},{18,... | collective-permute-start | bytes 968 | tf_op jit(solution)/shard_map/ppermute | solution.py:27
  27.3 3.7 %collective-permute-start.9 = (f32[5,4,4,1]{3,2,1,0:T(4,128)S(1)}, f32[5,4,4,1]{3,2,1,0:T(4,128)S(1)}, u32[]{:S(2)}, u32[]{:S(2)}) collective-permute-start(f32[5,4,4,1]{3,2,1,0:T(4,128)S(1)} %get-tuple-element.23), channel_id=1, source_target_pairs={{0,1},{1,0},{2,3},{3,2},{4,5},{5,4},{6,7},{7,6},{8,9},{9,8},{10,11... | collective-permute-start | bytes 968 | tf_op jit(solution)/shard_map/ppermute | solution.py:25
  31.1 0.9 %collective-permute-start.7 = (f32[5,4,1,128]{3,2,1,0:T(1,128)S(1)}, f32[5,4,1,128]{3,2,1,0:T(1,128)S(1)}, u32[]{:S(2)}, u32[]{:S(2)}) collective-permute-start(f32[5,4,1,128]{3,2,1,0:T(1,128)S(1)} %broadcast_select_fusion.10), channel_id=1, source_target_pairs={{0,4},{4,0},{1,5},{5,1},{2,6},{6,2},{3,7},{7,3},{8,12},{12,8},{9,1... | collective-permute-start | bytes 30728 | tf_op jit(solution)/shard_map/ppermute | solution.py:25
  32.0 0.5 collective-permute-start.6
  32.4 0.7 %collective-permute-start.5 = (f32[5,1,4,128]{3,2,1,0:T(4,128)S(1)}, f32[5,1,4,128]{3,2,1,0:T(4,128)S(1)}, u32[]{:S(2)}, u32[]{:S(2)}) collective-permute-start(f32[5,1,4,128]{3,2,1,0:T(4,128)S(1)} %get-tuple-element.21), channel_id=1, source_target_pairs={{8,16},{16,8},{9,17},{17,9},{10,18},{18,10},{11,19},{19,11},{12,20... | collective-permute-start | bytes 30728 | tf_op jit(solution)/shard_map/ppermute | solution.py:27
  33.1 1.6 %collective-permute-done.7 = f32[5,4,1,128]{3,2,1,0:T(1,128)S(1)} collective-permute-done((f32[5,4,1,128]{3,2,1,0:T(1,128)S(1)}, f32[5,4,1,128]{3,2,1,0:T(1,128)S(1)}, u32[]{:S(2)}, u32[]{:S(2)}) %collective-permute-start.7) | collective-permute-done | bytes 10272 | tf_op jit(solution)/shard_map/ppermute | solution.py:25
  34.8 0.2 fusion.26
  35.1 2.4 %convolution_bitcast_fusion = f32[3,16384,16]{1,2,0:T(8,128)S(1)} fusion(s32[16384]{0:T(1024)S(1)} %get-tuple-element.9, bf16[1,128,16]{1,2,0:T(8,128)(2,1)S(1)} %get-tuple-element.34, bf16[1,128,16]{1,2,0:T(8,128)(2,1)S(1)} %get-tuple-element.33, bf16[1,128,16]{1,2,0:T(8,128)(2,1)S(1)} %get-tuple-element.32), kind=kOutput, calls=%fused_computation | convolution fusion | flops 203436032 | bytes 3223552 | tf_op jit(solution)/shard_map/fd,kdp->kfp/dot_general | solution.py:89
  37.5 0.4 fusion.13
  37.9 11.5 %all_to_all.10 = f32[1,128,128]{2,0,1:T(1,128)S(1)} all-to-all(f32[1,128,128]{2,0,1:T(1,128)S(1)} %bitcast.85), channel_id=1, replica_groups=mesh['stream'=4,'cross'=2,'gore'=4] {'stream','cross'}, dimensions={1} | all-to-all | bytes 131072 | tf_op jit(solution)/shard_map/all_to_all | solution.py:160
  49.4 0.2 fusion.62
  49.6 0.7 %slice_multiply_fusion = f32[3,64,128]{2,1,0:T(8,128)} fusion(f32[8,64,128]{2,1,0:T(8,128)S(1)} %broadcast_select_fusion, f32[64,128]{1,0:T(8,128)S(1)} %fusion.62), kind=kLoop, calls=%fused_computation.27 | loop fusion | flops 24576 | bytes 229376 | tf_op jit(solution)/shard_map/mul | solution.py:170
  (37 shorter events, 0.7 us)
Async XLA Ops:
  6.2 15.3 %all-to-all-start = ((f32[6,128,128]{2,0,1:T(8,128)}), f32[6,128,128]{2,0,1:T(8,128)S(1)}, u32[]{:S(2)}, u32[]{:S(2)}) async-start(f32[6,128,128]{2,0,1:T(8,128)} %copy.11), calls=%async_computation | async-start | bytes 1048576 | tf_op jit(solution)/shard_map/all_to_all | solution.py:130
  12.3 7.9 %collective-permute-start.1 = (f32[6,4,4,1]{3,2,1,0:T(4,128)S(1)}, f32[6,4,4,1]{3,2,1,0:T(4,128)S(1)}, u32[]{:S(2)}, u32[]{:S(2)}) collective-permute-start(f32[6,4,4,1]{3,2,1,0:T(4,128)S(1)} %get-tuple-element.18), channel_id=1, source_target_pairs={{1,2},{2,1},{5,6},{6,5},{9,10},{10,9},{13,14},{14,13},{17,18},{18,... | collective-permute-start | bytes 1160 | tf_op jit(solution)/shard_map/ppermute | solution.py:27
  12.9 7.3 %collective-permute-start = (f32[6,4,4,1]{3,2,1,0:T(4,128)S(1)}, f32[6,4,4,1]{3,2,1,0:T(4,128)S(1)}, u32[]{:S(2)}, u32[]{:S(2)}) collective-permute-start(f32[6,4,4,1]{3,2,1,0:T(4,128)S(1)} %get-tuple-element.19), channel_id=1, source_target_pairs={{0,1},{1,0},{2,3},{3,2},{4,5},{5,4},{6,7},{7,6},{8,9},{9,8},{10,11... | collective-permute-start | bytes 1160 | tf_op jit(solution)/shard_map/ppermute | solution.py:25
  17.4 3.8 %collective-permute-start.2 = (f32[6,4,1,128]{3,2,1,0:T(1,128)S(1)}, f32[6,4,1,128]{3,2,1,0:T(1,128)S(1)}, u32[]{:S(2)}, u32[]{:S(2)}) collective-permute-start(f32[6,4,1,128]{3,2,1,0:T(1,128)S(1)} %broadcast_select_fusion.3), channel_id=1, source_target_pairs={{0,4},{4,0},{1,5},{5,1},{2,6},{6,2},{3,7},{7,3},{8,12},{12,8},{9,1... | collective-permute-start | bytes 36872 | tf_op jit(solution)/shard_map/ppermute | solution.py:25
  19.5 1.2 %collective-permute-start.3 = (f32[6,1,4,128]{3,2,1,0:T(4,128)S(1)}, f32[6,1,4,128]{3,2,1,0:T(4,128)S(1)}, u32[]{:S(2)}, u32[]{:S(2)}) collective-permute-start(f32[6,1,4,128]{3,2,1,0:T(4,128)S(1)} %get-tuple-element.16), channel_id=1, source_target_pairs={{0,8},{8,0},{16,24},{24,16},{1,9},{9,1},{17,25},{25,17},{2,10},{10... | collective-permute-start | bytes 36872 | tf_op jit(solution)/shard_map/ppermute | solution.py:25
  19.5 1.2 %collective-permute-start.4 = (f32[6,1,4,128]{3,2,1,0:T(4,128)S(1)}, f32[6,1,4,128]{3,2,1,0:T(4,128)S(1)}, u32[]{:S(2)}, u32[]{:S(2)}) collective-permute-start(f32[6,1,4,128]{3,2,1,0:T(4,128)S(1)} %get-tuple-element.17), channel_id=1, source_target_pairs={{8,16},{16,8},{9,17},{17,9},{10,18},{18,10},{11,19},{19,11},{12,20... | collective-permute-start | bytes 36872 | tf_op jit(solution)/shard_map/ppermute | solution.py:27
  26.6 6.4 %collective-permute-start.8 = (f32[5,4,4,1]{3,2,1,0:T(4,128)S(1)}, f32[5,4,4,1]{3,2,1,0:T(4,128)S(1)}, u32[]{:S(2)}, u32[]{:S(2)}) collective-permute-start(f32[5,4,4,1]{3,2,1,0:T(4,128)S(1)} %get-tuple-element.22), channel_id=1, source_target_pairs={{1,2},{2,1},{5,6},{6,5},{9,10},{10,9},{13,14},{14,13},{17,18},{18,... | collective-permute-start | bytes 968 | tf_op jit(solution)/shard_map/ppermute | solution.py:27
  27.3 5.8 %collective-permute-start.9 = (f32[5,4,4,1]{3,2,1,0:T(4,128)S(1)}, f32[5,4,4,1]{3,2,1,0:T(4,128)S(1)}, u32[]{:S(2)}, u32[]{:S(2)}) collective-permute-start(f32[5,4,4,1]{3,2,1,0:T(4,128)S(1)} %get-tuple-element.23), channel_id=1, source_target_pairs={{0,1},{1,0},{2,3},{3,2},{4,5},{5,4},{6,7},{7,6},{8,9},{9,8},{10,11... | collective-permute-start | bytes 968 | tf_op jit(solution)/shard_map/ppermute | solution.py:25
  31.1 3.7 %collective-permute-start.7 = (f32[5,4,1,128]{3,2,1,0:T(1,128)S(1)}, f32[5,4,1,128]{3,2,1,0:T(1,128)S(1)}, u32[]{:S(2)}, u32[]{:S(2)}) collective-permute-start(f32[5,4,1,128]{3,2,1,0:T(1,128)S(1)} %broadcast_select_fusion.10), channel_id=1, source_target_pairs={{0,4},{4,0},{1,5},{5,1},{2,6},{6,2},{3,7},{7,3},{8,12},{12,8},{9,1... | collective-permute-start | bytes 30728 | tf_op jit(solution)/shard_map/ppermute | solution.py:25
  32.0 2.8 %collective-permute-start.6 = (f32[5,1,4,128]{3,2,1,0:T(4,128)S(1)}, f32[5,1,4,128]{3,2,1,0:T(4,128)S(1)}, u32[]{:S(2)}, u32[]{:S(2)}) collective-permute-start(f32[5,1,4,128]{3,2,1,0:T(4,128)S(1)} %get-tuple-element.20), channel_id=1, source_target_pairs={{0,8},{8,0},{16,24},{24,16},{1,9},{9,1},{17,25},{25,17},{2,10},{10... | collective-permute-start | bytes 30728 | tf_op jit(solution)/shard_map/ppermute | solution.py:25
  32.4 2.4 %collective-permute-start.5 = (f32[5,1,4,128]{3,2,1,0:T(4,128)S(1)}, f32[5,1,4,128]{3,2,1,0:T(4,128)S(1)}, u32[]{:S(2)}, u32[]{:S(2)}) collective-permute-start(f32[5,1,4,128]{3,2,1,0:T(4,128)S(1)} %get-tuple-element.21), channel_id=1, source_target_pairs={{8,16},{16,8},{9,17},{17,9},{10,18},{18,10},{11,19},{19,11},{12,20... | collective-permute-start | bytes 30728 | tf_op jit(solution)/shard_map/ppermute | solution.py:27
  35.1 15.2 %copy-start = (f32[5,4,4,128]{3,2,1,0:T(4,128)}, f32[5,4,4,128]{3,2,1,0:T(4,128)S(1)}, u32[]{:S(2)}) copy-start(f32[5,4,4,128]{3,2,1,0:T(4,128)S(1)} %fusion.26) | copy-start | bytes 122884
where the time goes:
time: 50.8 us; the launch traced here: 50.3 us
  starting transfers between devices  19.5 us (38%)
  blocking collectives  11.5 us (23%)
  matrix products  7.97 us (16%)
  other arithmetic  6.61 us (13%)
  waiting for transfers between devices  2.53 us (5%)
  local copies, waits for them, and re-layouts  1.21 us (2%)
  between operations  1 us (2%)
    ppermute x6, starting transfers between devices, face_halo(): from_a = lax.ppermute(jnp.where(odd, first, last), axis, pairs_a)  11.6 us
    all_to_all x1, blocking collectives, shards(): lax.all_to_all(face_pressure.reshape(1, slot_total, row_count), ('stream'...  11.5 us
    all_to_all x1, starting transfers between devices, shards(): lax.all_to_all(outbound, ('stream', 'cross'), split_axis=1, concat_axis=1...  5.17 us
    dot_general x1, matrix products, shards(): jnp.einsum('cpf,fd->cpd', spread, depth_hot.astype(jnp.float32), precisio...  3.97 us
    ppermute x4, starting transfers between devices, face_halo(): from_b = lax.ppermute(jnp.where(odd, last, first), axis, pairs_b)  2.64 us
    ppermute x6, waiting for transfers between devices, face_halo(): from_a = lax.ppermute(jnp.where(odd, first, last), axis, pairs_a)  2.52 us
    dot_general x1, matrix products, exact_dot(): jnp.einsum(left + ',k' + right + '->k' + output, onehot, stacked, preferr...  2.4 us
  transfers between devices with their start and end apart: 11, of which 3 were waited for; matrix products, arithmetic and copies ran while one was open for 3% of the time, Pallas kernels for 0%

commit v1 on v0

--- a/solution.py
+++ b/solution.py
@@ -127,7 +127,15 @@
         [jnp.abs(masked_values[0:1]), masked_values[1:5], cell_ids.astype(jnp.float32)[None]], 0
     )
     outbound = jnp.einsum("ts,ctr->csr", placement_plan, payload, precision=lax.Precision.HIGHEST)
-    arrived = lax.all_to_all(outbound, ("stream", "cross"), split_axis=1, concat_axis=1, tiled=True)
+    arrived = jnp.concatenate(
+        lax.all_to_all(
+            jnp.stack(jnp.split(outbound, lax.axis_size(("stream", "cross")), axis=1)),
+            ("stream", "cross"),
+            0,
+            0,
+        ),
+        axis=1,
+    )
     outbound, state_and_visc = lax.optimization_barrier(
         (outbound, jnp.concatenate([fluid_state, viscosity[None]], 0))
     )

time: 50.8 us -> 54.8 us (1.079)
  local copies, waits for them, and re-layouts: 1.21 us -> 5.3 us
  waiting for transfers between devices: 2.53 us -> 1.12 us
  blocking collectives: 11.5 us -> 12.9 us
    unnamed x2 -> x10, local copies, waits for them, and re-layouts: 0.01 us -> 4.53 us
    ppermute x6, waiting for transfers between devices: 2.52 us -> 1.11 us  [face_halo(): from_a = lax.ppermute(jnp.where(odd, first, last), axis, pairs_a)]
    all_to_all x1, blocking collectives: 11.5 us -> 12.9 us  [shards(): lax.all_to_all(face_pressure.reshape(1, slot_total, row_count), ('stream'...]
    transpose x1 -> x0, local copies, waits for them, and re-layouts: 0.99 us -> none  [shards(): jnp.einsum('ts,ctr->csr', placement_plan, payload, precision=lax.Precisio...]
    another operation x0 -> x1, local copies, waits for them, and re-layouts: none -> 0.62 us  [shards(): jnp.stack(jnp.split(outbound, lax.axis_size(('stream', 'cross')), axis=1))]
  transfers between devices with their start and end apart: 11 -> 11, of which waited for: 3 -> 3; matrix products, arithmetic and copies ran while one was open for 3% -> 2% of each run, Pallas kernels for 0% -> 0%
where the time goes in v1:
time: 54.8 us; the launch traced here: 54.3 us
  starting transfers between devices  19.5 us (36%)
  blocking collectives  12.9 us (24%)
  matrix products  7.89 us (14%)
  other arithmetic  6.63 us (12%)
  local copies, waits for them, and re-layouts  5.3 us (10%)
  waiting for transfers between devices  1.12 us (2%)
  between operations  1.02 us (2%)
    all_to_all x1, blocking collectives, shards(): lax.all_to_all(face_pressure.reshape(1, slot_total, row_count), ('stream'...  12.9 us
    ppermute x6, starting transfers between devices, face_halo(): from_a = lax.ppermute(jnp.where(odd, first, last), axis, pairs_a)  11.6 us
    all_to_all x1, starting transfers between devices, shards(): lax.all_to_all(jnp.stack(jnp.split(outbound, lax.axis_size(('stream', 'cr...  5.17 us
    unnamed x10, local copies, waits for them, and re-layouts  4.53 us
    dot_general x1, matrix products, shards(): jnp.einsum('cpf,fd->cpd', spread, depth_hot.astype(jnp.float32), precisio...  3.98 us
    ppermute x4, starting transfers between devices, face_halo(): from_b = lax.ppermute(jnp.where(odd, last, first), axis, pairs_b)  2.64 us
    dot_general x1, matrix products, exact_dot(): jnp.einsum(left + ',k' + right + '->k' + output, onehot, stacked, preferr...  2.4 us
    ppermute x6, waiting for transfers between devices, face_halo(): from_a = lax.ppermute(jnp.where(odd, first, last), axis, pairs_a)  1.11 us
  transfers between devices with their start and end apart: 11, of which 3 were waited for; matrix products, arithmetic and copies ran while one was open for 2% of the time, Pallas kernels for 0%

profile of v1, /device:TPU:0, one launch (start us, length us, event | category | flops | bytes accessed | tf_op | source)
XLA Modules:
  0.0 54.3 jit_solution(16620309989094737712)
XLA Ops:
  0.6 0.7 %iota_compare_fusion.6 = pred[64,128]{1,0:T(8,128)(4,1)S(1)} fusion(s32[64]{0:T(128)} %param.13), kind=kLoop, calls=%fused_computation.149 | loop fusion | flops 8192 | bytes 8448 | tf_op jit(solution)/shard_map/lt | solution.py:108
  1.4 1.0 %broadcast_select_fusion = f32[8,64,128]{2,1,0:T(8,128)S(1)} fusion(f32[8,64,128]{2,1,0:T(8,128)} %param.10, pred[64,128]{1,0:T(8,128)(4,1)S(1)} %iota_compare_fusion.6), kind=kLoop, calls=%fused_computation.26 | loop fusion | flops 65536 | bytes 532480 | tf_op jit(solution)/shard_map/jit(_where)/select_n | solution.py:109
  2.4 0.8 %convert_bitcast_fusion = f32[1,64,128]{2,1,0:T(8,128)S(1)} fusion(s32[64,128]{1,0:T(8,128)} %param.11), kind=kLoop, calls=%fused_computation.148 | loop fusion | flops 8192 | bytes 65536 | tf_op jit(solution)/shard_map/broadcast_in_dim | solution.py:127
  3.1 0.9 %fusion.10 = f32[64]{0:T(128)S(1)} fusion(s32[64]{0:T(128)} %bitcast.113), kind=kOutput, calls=%fused_computation.12 | convolution fusion | flops 71616 | bytes 512 | tf_op jit(solution)/shard_map/dot_general | solution.py:118
  4.0 0.7 %fusion.100 = s32[64]{0:T(128)S(1)} fusion(f32[64]{0:T(128)S(1)} %fusion.10, s32[64,1]{0,1:T(1,128)} %param.12), kind=kLoop, calls=%fused_computation.210 | loop fusion | flops 192 | bytes 768 | tf_op jit(solution)/shard_map/eq | solution.py:124
  4.7 0.4 convolution_bitcast_fusion.1
  5.1 0.6 %fusion.28 = f32[8,6,16,128]{3,2,1,0:T(8,128)} fusion(f32[6,128,128]{2,1,0:T(8,128)S(1)} %convolution_bitcast_fusion.1), kind=kLoop, calls=%fused_computation.52 | loop fusion | bytes 98304
  5.7 0.6 %fusion.27 = f32[8,6,16,128]{3,2,1,0:T(8,128)} fusion(f32[8,6,16,128]{3,2,1,0:T(8,128)} %fusion.28, f32[6,128,128]{2,1,0:T(8,128)S(1)} %convolution_bitcast_fusion.1), kind=kLoop, calls=%fused_computation.50 | loop fusion | bytes 98304
  6.4 0.6 %fusion.26 = f32[8,6,16,128]{3,2,1,0:T(8,128)} fusion(f32[8,6,16,128]{3,2,1,0:T(8,128)} %fusion.27, f32[6,128,128]{2,1,0:T(8,128)S(1)} %convolution_bitcast_fusion.1), kind=kLoop, calls=%fused_computation.48 | loop fusion | bytes 98304
  7.0 0.6 %fusion.25 = f32[8,6,16,128]{3,2,1,0:T(8,128)} fusion(f32[8,6,16,128]{3,2,1,0:T(8,128)} %fusion.26, f32[6,128,128]{2,1,0:T(8,128)S(1)} %convolution_bitcast_fusion.1), kind=kLoop, calls=%fused_computation.46 | loop fusion | bytes 98304
  7.6 0.6 %fusion.24 = f32[8,6,16,128]{3,2,1,0:T(8,128)} fusion(f32[8,6,16,128]{3,2,1,0:T(8,128)} %fusion.25, f32[6,128,128]{2,1,0:T(8,128)S(1)} %convolution_bitcast_fusion.1), kind=kLoop, calls=%fused_computation.44 | loop fusion | bytes 98304
  8.2 0.6 %fusion.23 = f32[8,6,16,128]{3,2,1,0:T(8,128)} fusion(f32[8,6,16,128]{3,2,1,0:T(8,128)} %fusion.24, f32[6,128,128]{2,1,0:T(8,128)S(1)} %convolution_bitcast_fusion.1), kind=kLoop, calls=%fused_computation.42 | loop fusion | bytes 98304
  8.8 0.6 %fusion.22 = f32[8,6,16,128]{3,2,1,0:T(8,128)} fusion(f32[8,6,16,128]{3,2,1,0:T(8,128)} %fusion.23, f32[6,128,128]{2,1,0:T(8,128)S(1)} %convolution_bitcast_fusion.1), kind=kLoop, calls=%fused_computation.40 | loop fusion | bytes 98304
  9.4 0.6 %fusion.21 = f32[8,6,16,128]{3,2,1,0:T(8,128)} fusion(f32[8,6,16,128]{3,2,1,0:T(8,128)} %fusion.22, f32[6,128,128]{2,1,0:T(8,128)S(1)} %convolution_bitcast_fusion.1), kind=kLoop, calls=%fused_computation.38 | loop fusion | bytes 98304 | tf_op jit(solution)/shard_map/stack | solution.py:132
  10.1 5.2 %all-to-all-start = ((f32[8,6,16,128]{3,2,1,0:T(8,128)}), f32[8,6,16,128]{3,2,1,0:T(8,128)S(1)}, u32[]{:S(2)}, u32[]{:S(2)}) async-start(f32[8,6,16,128]{3,2,1,0:T(8,128)} %fusion.21), calls=%async_computation | async-start | bytes 786432 | tf_op jit(solution)/shard_map/all_to_all | solution.py:131
  15.2 0.8 %pad_maximum_fusion.6 = f32[6,4,4,128]{3,2,1,0:T(4,128)S(1)} fusion(f32[1,4,4,128]{3,2,1,0:T(4,128)} %bitcast.111, f32[4,4,4,128]{3,2,1,0:T(4,128)} %param.8, f32[1,4,4,128]{3,2,1,0:T(4,128)} %bitcast.112), kind=kLoop, calls=%fused_computation.60 | loop fusion | flops 24576 | bytes 98304 | tf_op jit(solution)/shard_map/concatenate | solution.py:140
  16.1 0.7 %collective-permute-start.1 = (f32[6,4,4,1]{3,2,1,0:T(4,128)S(1)}, f32[6,4,4,1]{3,2,1,0:T(4,128)S(1)}, u32[]{:S(2)}, u32[]{:S(2)}) collective-permute-start(f32[6,4,4,1]{3,2,1,0:T(4,128)S(1)} %get-tuple-element.18), channel_id=1, source_target_pairs={{1,2},{2,1},{5,6},{6,5},{9,10},{10,9},{13,14},{14,13},{17,18},{18,... | collective-permute-start | bytes 1160 | tf_op jit(solution)/shard_map/ppermute | solution.py:27
  16.8 4.5 %collective-permute-start = (f32[6,4,4,1]{3,2,1,0:T(4,128)S(1)}, f32[6,4,4,1]{3,2,1,0:T(4,128)S(1)}, u32[]{:S(2)}, u32[]{:S(2)}) collective-permute-start(f32[6,4,4,1]{3,2,1,0:T(4,128)S(1)} %get-tuple-element.19), channel_id=1, source_target_pairs={{0,1},{1,0},{2,3},{3,2},{4,5},{5,4},{6,7},{7,6},{8,9},{9,8},{10,11... | collective-permute-start | bytes 1160 | tf_op jit(solution)/shard_map/ppermute | solution.py:25
  21.3 2.1 %collective-permute-start.2 = (f32[6,4,1,128]{3,2,1,0:T(1,128)S(1)}, f32[6,4,1,128]{3,2,1,0:T(1,128)S(1)}, u32[]{:S(2)}, u32[]{:S(2)}) collective-permute-start(f32[6,4,1,128]{3,2,1,0:T(1,128)S(1)} %broadcast_select_fusion.3), channel_id=1, source_target_pairs={{0,4},{4,0},{1,5},{5,1},{2,6},{6,2},{3,7},{7,3},{8,12},{12,8},{9,1... | collective-permute-start | bytes 36872 | tf_op jit(solution)/shard_map/ppermute | solution.py:25
  23.4 0.7 %collective-permute-start.4 = (f32[6,1,4,128]{3,2,1,0:T(4,128)S(1)}, f32[6,1,4,128]{3,2,1,0:T(4,128)S(1)}, u32[]{:S(2)}, u32[]{:S(2)}) collective-permute-start(f32[6,1,4,128]{3,2,1,0:T(4,128)S(1)} %get-tuple-element.17), channel_id=1, source_target_pairs={{8,16},{16,8},{9,17},{17,9},{10,18},{18,10},{11,19},{19,11},{12,20... | collective-permute-start | bytes 36872 | tf_op jit(solution)/shard_map/ppermute | solution.py:27
  24.2 0.4 collective-permute-done.3
  24.6 0.5 collective-permute-done.2
  25.9 0.5 fusion.111
  26.3 4.0 %fusion.2 = f32[5,16,128]{2,1,0:T(8,128)S(1)} fusion(s32[16384]{0:T(1024)S(1)} %get-tuple-element.9, f32[5,16,16384]{2,1,0:T(8,128)S(1)} %fusion.111), kind=kOutput, calls=%fused_computation.3 | convolution fusion | flops 2015363072 | bytes 5349376 | tf_op jit(solution)/shard_map/cpf,fd->cpd/dot_general | solution.py:151
  30.7 0.7 %collective-permute-start.8 = (f32[5,4,4,1]{3,2,1,0:T(4,128)S(1)}, f32[5,4,4,1]{3,2,1,0:T(4,128)S(1)}, u32[]{:S(2)}, u32[]{:S(2)}) collective-permute-start(f32[5,4,4,1]{3,2,1,0:T(4,128)S(1)} %get-tuple-element.22), channel_id=1, source_target_pairs={{1,2},{2,1},{5,6},{6,5},{9,10},{10,9},{13,14},{14,13},{17,18},{18,... | collective-permute-start | bytes 968 | tf_op jit(solution)/shard_map/ppermute | solution.py:27
  31.4 2.3 %collective-permute-start.9 = (f32[5,4,4,1]{3,2,1,0:T(4,128)S(1)}, f32[5,4,4,1]{3,2,1,0:T(4,128)S(1)}, u32[]{:S(2)}, u32[]{:S(2)}) collective-permute-start(f32[5,4,4,1]{3,2,1,0:T(4,128)S(1)} %get-tuple-element.23), channel_id=1, source_target_pairs={{0,1},{1,0},{2,3},{3,2},{4,5},{5,4},{6,7},{7,6},{8,9},{9,8},{10,11... | collective-permute-start | bytes 968 | tf_op jit(solution)/shard_map/ppermute | solution.py:25
  33.7 1.9 %collective-permute-start.7 = (f32[5,4,1,128]{3,2,1,0:T(1,128)S(1)}, f32[5,4,1,128]{3,2,1,0:T(1,128)S(1)}, u32[]{:S(2)}, u32[]{:S(2)}) collective-permute-start(f32[5,4,1,128]{3,2,1,0:T(1,128)S(1)} %broadcast_select_fusion.10), channel_id=1, source_target_pairs={{0,4},{4,0},{1,5},{5,1},{2,6},{6,2},{3,7},{7,3},{8,12},{12,8},{9,1... | collective-permute-start | bytes 30728 | tf_op jit(solution)/shard_map/ppermute | solution.py:25
  35.6 0.9 %collective-permute-start.6 = (f32[5,1,4,128]{3,2,1,0:T(4,128)S(1)}, f32[5,1,4,128]{3,2,1,0:T(4,128)S(1)}, u32[]{:S(2)}, u32[]{:S(2)}) collective-permute-start(f32[5,1,4,128]{3,2,1,0:T(4,128)S(1)} %get-tuple-element.20), channel_id=1, source_target_pairs={{0,8},{8,0},{16,24},{24,16},{1,9},{9,1},{17,25},{25,17},{2,10},{10... | collective-permute-start | bytes 30728 | tf_op jit(solution)/shard_map/ppermute | solution.py:25
  36.4 0.7 %collective-permute-start.5 = (f32[5,1,4,128]{3,2,1,0:T(4,128)S(1)}, f32[5,1,4,128]{3,2,1,0:T(4,128)S(1)}, u32[]{:S(2)}, u32[]{:S(2)}) collective-permute-start(f32[5,1,4,128]{3,2,1,0:T(4,128)S(1)} %get-tuple-element.21), channel_id=1, source_target_pairs={{8,16},{16,8},{9,17},{17,9},{10,18},{18,10},{11,19},{19,11},{12,20... | collective-permute-start | bytes 30728 | tf_op jit(solution)/shard_map/ppermute | solution.py:27
  37.7 2.4 %convolution_bitcast_fusion = f32[3,16384,16]{1,2,0:T(8,128)S(1)} fusion(s32[16384]{0:T(1024)S(1)} %get-tuple-element.9, bf16[1,128,16]{1,2,0:T(8,128)(2,1)S(1)} %get-tuple-element.34, bf16[1,128,16]{1,2,0:T(8,128)(2,1)S(1)} %get-tuple-element.33, bf16[1,128,16]{1,2,0:T(8,128)(2,1)S(1)} %get-tuple-element.32), kind=kOutput, calls=%fused_computation | convolution fusion | flops 203436032 | bytes 3223552 | tf_op jit(solution)/shard_map/fd,kdp->kfp/dot_general | solution.py:89
  40.5 12.9 %all_to_all.10 = f32[1,128,128]{2,0,1:T(1,128)S(1)} all-to-all(f32[1,128,128]{2,0,1:T(1,128)S(1)} %bitcast.99), channel_id=1, replica_groups=mesh['stream'=4,'cross'=2,'gore'=4] {'stream','cross'}, dimensions={1} | all-to-all | bytes 131072 | tf_op jit(solution)/shard_map/all_to_all | solution.py:168
  53.6 0.7 %slice_multiply_fusion = f32[3,64,128]{2,1,0:T(8,128)} fusion(f32[8,64,128]{2,1,0:T(8,128)S(1)} %broadcast_select_fusion, f32[64,128]{1,0:T(8,128)S(1)} %fusion.70), kind=kLoop, calls=%fused_computation.27 | loop fusion | flops 24576 | bytes 229376 | tf_op jit(solution)/shard_map/mul | solution.py:178
  (46 shorter events, 2.4 us)
Async XLA Ops:
  10.1 15.3 %all-to-all-start = ((f32[8,6,16,128]{3,2,1,0:T(8,128)}), f32[8,6,16,128]{3,2,1,0:T(8,128)S(1)}, u32[]{:S(2)}, u32[]{:S(2)}) async-start(f32[8,6,16,128]{3,2,1,0:T(8,128)} %fusion.21), calls=%async_computation | async-start | bytes 786432 | tf_op jit(solution)/shard_map/all_to_all | solution.py:131
  16.1 7.9 %collective-permute-start.1 = (f32[6,4,4,1]{3,2,1,0:T(4,128)S(1)}, f32[6,4,4,1]{3,2,1,0:T(4,128)S(1)}, u32[]{:S(2)}, u32[]{:S(2)}) collective-permute-start(f32[6,4,4,1]{3,2,1,0:T(4,128)S(1)} %get-tuple-element.18), channel_id=1, source_target_pairs={{1,2},{2,1},{5,6},{6,5},{9,10},{10,9},{13,14},{14,13},{17,18},{18,... | collective-permute-start | bytes 1160 | tf_op jit(solution)/shard_map/ppermute | solution.py:27
  16.8 7.3 %collective-permute-start = (f32[6,4,4,1]{3,2,1,0:T(4,128)S(1)}, f32[6,4,4,1]{3,2,1,0:T(4,128)S(1)}, u32[]{:S(2)}, u32[]{:S(2)}) collective-permute-start(f32[6,4,4,1]{3,2,1,0:T(4,128)S(1)} %get-tuple-element.19), channel_id=1, source_target_pairs={{0,1},{1,0},{2,3},{3,2},{4,5},{5,4},{6,7},{7,6},{8,9},{9,8},{10,11... | collective-permute-start | bytes 1160 | tf_op jit(solution)/shard_map/ppermute | solution.py:25
  21.3 3.8 %collective-permute-start.2 = (f32[6,4,1,128]{3,2,1,0:T(1,128)S(1)}, f32[6,4,1,128]{3,2,1,0:T(1,128)S(1)}, u32[]{:S(2)}, u32[]{:S(2)}) collective-permute-start(f32[6,4,1,128]{3,2,1,0:T(1,128)S(1)} %broadcast_select_fusion.3), channel_id=1, source_target_pairs={{0,4},{4,0},{1,5},{5,1},{2,6},{6,2},{3,7},{7,3},{8,12},{12,8},{9,1... | collective-permute-start | bytes 36872 | tf_op jit(solution)/shard_map/ppermute | solution.py:25
  23.4 1.2 %collective-permute-start.3 = (f32[6,1,4,128]{3,2,1,0:T(4,128)S(1)}, f32[6,1,4,128]{3,2,1,0:T(4,128)S(1)}, u32[]{:S(2)}, u32[]{:S(2)}) collective-permute-start(f32[6,1,4,128]{3,2,1,0:T(4,128)S(1)} %get-tuple-element.16), channel_id=1, source_target_pairs={{0,8},{8,0},{16,24},{24,16},{1,9},{9,1},{17,25},{25,17},{2,10},{10... | collective-permute-start | bytes 36872 | tf_op jit(solution)/shard_map/ppermute | solution.py:25
  23.4 1.2 %collective-permute-start.4 = (f32[6,1,4,128]{3,2,1,0:T(4,128)S(1)}, f32[6,1,4,128]{3,2,1,0:T(4,128)S(1)}, u32[]{:S(2)}, u32[]{:S(2)}) collective-permute-start(f32[6,1,4,128]{3,2,1,0:T(4,128)S(1)} %get-tuple-element.17), channel_id=1, source_target_pairs={{8,16},{16,8},{9,17},{17,9},{10,18},{18,10},{11,19},{19,11},{12,20... | collective-permute-start | bytes 36872 | tf_op jit(solution)/shard_map/ppermute | solution.py:27
  30.7 6.4 %collective-permute-start.8 = (f32[5,4,4,1]{3,2,1,0:T(4,128)S(1)}, f32[5,4,4,1]{3,2,1,0:T(4,128)S(1)}, u32[]{:S(2)}, u32[]{:S(2)}) collective-permute-start(f32[5,4,4,1]{3,2,1,0:T(4,128)S(1)} %get-tuple-element.22), channel_id=1, source_target_pairs={{1,2},{2,1},{5,6},{6,5},{9,10},{10,9},{13,14},{14,13},{17,18},{18,... | collective-permute-start | bytes 968 | tf_op jit(solution)/shard_map/ppermute | solution.py:27
  31.4 5.8 %collective-permute-start.9 = (f32[5,4,4,1]{3,2,1,0:T(4,128)S(1)}, f32[5,4,4,1]{3,2,1,0:T(4,128)S(1)}, u32[]{:S(2)}, u32[]{:S(2)}) collective-permute-start(f32[5,4,4,1]{3,2,1,0:T(4,128)S(1)} %get-tuple-element.23), channel_id=1, source_target_pairs={{0,1},{1,0},{2,3},{3,2},{4,5},{5,4},{6,7},{7,6},{8,9},{9,8},{10,11... | collective-permute-start | bytes 968 | tf_op jit(solution)/shard_map/ppermute | solution.py:25
  33.7 3.7 %collective-permute-start.7 = (f32[5,4,1,128]{3,2,1,0:T(1,128)S(1)}, f32[5,4,1,128]{3,2,1,0:T(1,128)S(1)}, u32[]{:S(2)}, u32[]{:S(2)}) collective-permute-start(f32[5,4,1,128]{3,2,1,0:T(1,128)S(1)} %broadcast_select_fusion.10), channel_id=1, source_target_pairs={{0,4},{4,0},{1,5},{5,1},{2,6},{6,2},{3,7},{7,3},{8,12},{12,8},{9,1... | collective-permute-start | bytes 30728 | tf_op jit(solution)/shard_map/ppermute | solution.py:25
  35.6 1.9 %collective-permute-start.6 = (f32[5,1,4,128]{3,2,1,0:T(4,128)S(1)}, f32[5,1,4,128]{3,2,1,0:T(4,128)S(1)}, u32[]{:S(2)}, u32[]{:S(2)}) collective-permute-start(f32[5,1,4,128]{3,2,1,0:T(4,128)S(1)} %get-tuple-element.20), channel_id=1, source_target_pairs={{0,8},{8,0},{16,24},{24,16},{1,9},{9,1},{17,25},{25,17},{2,10},{10... | collective-permute-start | bytes 30728 | tf_op jit(solution)/shard_map/ppermute | solution.py:25
  36.4 1.0 %collective-permute-start.5 = (f32[5,1,4,128]{3,2,1,0:T(4,128)S(1)}, f32[5,1,4,128]{3,2,1,0:T(4,128)S(1)}, u32[]{:S(2)}, u32[]{:S(2)}) collective-permute-start(f32[5,1,4,128]{3,2,1,0:T(4,128)S(1)} %get-tuple-element.21), channel_id=1, source_target_pairs={{8,16},{16,8},{9,17},{17,9},{10,18},{18,10},{11,19},{19,11},{12,20... | collective-permute-start | bytes 30728 | tf_op jit(solution)/shard_map/ppermute | solution.py:27
  37.7 16.6 %copy-start = (f32[5,4,4,128]{3,2,1,0:T(4,128)}, f32[5,4,4,128]{3,2,1,0:T(4,128)S(1)}, u32[]{:S(2)}) copy-start(f32[5,4,4,128]{3,2,1,0:T(4,128)S(1)} %fusion.35) | copy-start | bytes 122884
